TPU v7x, 32 devices: a whole 2x2x4 slice. The times are simulated.
32 devices in a mesh: box: 8 (over z, y), rep: 4 (over x, core).
Axes of the slice: x: 2, y: 2, z: 4, core: 2. Of those that a mesh axis runs over, the one named last changes fastest.
Arguments:
- targets: float32 [128, 256], P('box'), may hold values from -6 to 6
- noise_var: float32 [128, 256], P('box'), may hold values from 1 to 4
- near_tiles: bfloat16 [128, 8, 256, 256], P('box', 'rep'), may hold values from -1 to 1
- near_partners: int32 [128, 8], P('box', 'rep'), may hold values from -1 to 127, as said below
- leaf_bases: bfloat16 [128, 64, 256], P('box'), may hold values from -0.375 to 0.375
- transfer: bfloat16 [128, 64, 64], P('box'), may hold values from -0.375 to 0.375
- parents: int32 [128], P('box'), may hold values from 0 to 31, as said below
- coupling: bfloat16 [160, 16, 64, 64], P('box', 'rep'), may hold values from -0.109375 to 0.109375
- coupling_partners: int32 [160, 16], P('box', 'rep'), may hold values from -1 to 159, as said below
Outputs:
- weights: float32 [128, 256], P('box')
- residual: float32 [128, 256], P('box')
Inputs may be any that keep to these rules, and one draw needn't show every extreme that they name: `near_partners`: the first slot of each box's row is the box itself; every other entry is -1 or a box at most 16 boxes after the row's box. `coupling_partners`: each entry is -1 or a node of the same level as the row's node (leaf box or parent) with a higher number. The parents of the boxes of one index of box are that index's 4 parents. Along those boxes the parent number never decreases, so each parent's children are one contiguous run of one box or more.
All inputs are finite; a program needn't handle non-finite values.
Results may differ from a plain program's by a relative error of at most 0.006.
Values may be sent and summed in bfloat16 or wider, within the bound.
No kernel may reach another device: no remote copies, remote signals or barrier semaphores. Data moves between devices by JAX's collectives and lax.ppermute only.
A program may use at most 64 MiB of HBM per device.

v0:
```python
import jax
import jax.numpy as jnp
from jax import lax
from jax.sharding import PartitionSpec as P

ITERS = 2


def shifted(shard, axis, by):
    devices = lax.axis_size(axis)
    pairs = [(i, i + by) for i in range(devices) if 0 <= i + by < devices]
    return lax.ppermute(shard, axis, pairs)


def local(
    targets,
    noise_var,
    near_tiles,
    near_partners,
    leaf_bases,
    transfer,
    parents,
    coupling,
    coupling_partners,
):
    box_count = targets.shape[0]
    node_count = coupling.shape[0]
    group_count = node_count - box_count
    rank_width = coupling.shape[2]
    box_rank = lax.axis_index("box")
    all_nodes = lax.axis_size("box") * node_count
    near_valid = near_partners >= 0
    near_local = jnp.where(near_valid, near_partners - box_rank * box_count, 0)
    near_onehot = (
        (jnp.arange(2 * box_count, dtype=jnp.int32)[:, None] == near_local.reshape(1, -1))
        & near_valid.reshape(1, -1)
    ).astype(jnp.float32)
    parent_local = parents - box_rank * group_count
    parent_onehot = (
        jnp.arange(group_count, dtype=jnp.int32)[:, None] == parent_local[None, :]
    ).astype(jnp.float32)
    far_valid = coupling_partners >= 0
    far_index = jnp.where(far_valid, coupling_partners, 0)
    bf_zero = jnp.zeros((), jnp.bfloat16)

    def squares(vector):
        return lax.psum(jnp.sum(vector * vector), "box")

    weights = jnp.zeros_like(targets)
    residual = targets
    direction = targets
    norm_now = squares(residual)
    for iteration in range(ITERS):
        rounded = direction.astype(jnp.bfloat16)
        following = shifted(rounded, "box", -1)
        extended = jnp.concatenate([rounded, following], axis=0)
        near_in = jnp.where(near_valid[:, :, None], extended[near_local], bf_zero)
        forward = jnp.einsum(
            "bsij,bsj->bi", near_tiles, near_in, preferred_element_type=jnp.float32
        )
        mirrored = jnp.einsum(
            "bsij,bi->bsj", near_tiles, rounded, preferred_element_type=jnp.float32
        )
        landed = jnp.dot(
            near_onehot, mirrored.reshape(-1, mirrored.shape[2]), precision=lax.Precision.HIGHEST
        )
        arrived = shifted(landed[box_count:], "box", 1)
        near_part = forward + landed[:box_count] + arrived
        leaf_coef = jnp.einsum(
            "brl,bl->br", leaf_bases, rounded, preferred_element_type=jnp.float32
        ).astype(jnp.bfloat16)
        upward = jnp.einsum("brq,br->bq", transfer, leaf_coef, preferred_element_type=jnp.float32)
        group_coef = jnp.dot(parent_onehot, upward, precision=lax.Precision.HIGHEST).astype(
            jnp.bfloat16
        )
        node_coef = jnp.concatenate([leaf_coef, group_coef], axis=0)
        every_coef = lax.all_gather(node_coef, "box", axis=0, tiled=True)
        partner_coef = jnp.where(far_valid[:, :, None], every_coef[far_index], bf_zero)
        far_forward = jnp.einsum(
            "nsab,nsb->na", coupling, partner_coef, preferred_element_type=jnp.float32
        )
        far_mirror = jnp.einsum(
            "nsab,na->nsb", coupling, node_coef, preferred_element_type=jnp.float32
        )
        far_mirror = far_mirror * far_valid[:, :, None].astype(jnp.float32)
        spread = (
            jnp.zeros((all_nodes, rank_width), jnp.float32)
            .at[far_index.reshape(-1)]
            .add(far_mirror.reshape(-1, rank_width))
        )
        node_sums = lax.psum_scatter(spread, "box", scatter_dimension=0, tiled=True)
        near_total, far_total = lax.psum((near_part, node_sums + far_forward), "rep")
        group_out = far_total[box_count:].astype(jnp.bfloat16)
        from_parent = jnp.einsum(
            "brq,bq->br", transfer, group_out[parent_local], preferred_element_type=jnp.float32
        )
        downward = (far_total[:box_count] + from_parent).astype(jnp.bfloat16)
        far_field = jnp.einsum(
            "brl,br->bl", leaf_bases, downward, preferred_element_type=jnp.float32
        )
        image_vec = noise_var * direction + near_total + far_field
        step_size = norm_now / lax.psum(jnp.sum(direction * image_vec), "box")
        weights = weights + step_size * direction
        residual = residual - step_size * image_vec
        norm_next = squares(residual)
        direction = residual + norm_next / norm_now * direction
        norm_now = norm_next
    return (weights, residual)


def solution(mesh):
    placed = (
        P("box", None),
        P("box", None),
        P("box", "rep", None, None),
        P("box", "rep"),
        P("box", None, None),
        P("box", None, None),
        P("box"),
        P("box", "rep", None, None),
        P("box", "rep"),
    )
    return jax.shard_map(
        local,
        mesh=mesh,
        in_specs=placed,
        out_specs=(P("box", None), P("box", None)),
        check_vma=False,
    )
```

profile of v0, /device:TPU:0, one launch (start us, length us, event | category | flops | bytes accessed | tf_op | source)
XLA Modules:
  0.0 256.1 jit_solution(12259696300122468750)
XLA Ops:
  0.7 0.9 convert_bitcast_fusion.1
  1.6 2.8 %fusion.22 = f32[16,1,2,256]{3,1,2,0:T(1,128)S(1)} fusion(bf16[16,2,256,256]{3,2,1,0:T(8,128)(2,1)} %param.11, bf16[16,256,1,1]{1,0,2,3:T(8,128)(2,1)S(1)} %convert_bitcast_fusion.1), kind=kOutput, calls=%fused_computation.46 | convolution fusion | flops 4194304 | bytes 4235264 | tf_op jit(solution)/shard_map/bsij,bi->bsj/dot_general | solution.py:61
  4.5 0.1 copy.29
  4.6 0.1 eq.29
  4.7 0.1 copy.27
  4.8 0.1 and.11
  4.9 0.1 fusion.27
  5.1 4.9 %collective-permute-start.1 = (f32[16,256]{1,0:T(8,128)S(1)}, f32[16,256]{1,0:T(8,128)S(1)}, u32[]{:S(2)}, u32[]{:S(2)}) collective-permute-start(f32[16,256]{1,0:T(8,128)S(1)} %slice.47), channel_id=1, source_target_pairs={{0,4},{4,8},{8,12},{12,16},{16,20},{20,24},{24,28},{1,5},{5,9},{9,... | collective-permute-start | bytes 49160 | tf_op jit(solution)/shard_map/ppermute | solution.py:12
  10.0 1.3 collective-permute-start
  11.3 0.2 fusion.20
  11.6 0.1 copy.33
  11.7 0.1 copy.31
  11.8 0.1 reshape.58
  11.9 0.1 copy.32
  12.0 0.2 fusion.45
  12.2 0.1 convolution_convert_fusion.1
  12.3 0.3 fusion.31
  12.6 0.1 broadcast_multiply_fusion.1
  12.7 0.9 scatter_custom_fusion
  13.6 39.5 %all-reduce = f32[160,64]{1,0:T(8,128)S(1)} all-reduce(f32[160,64]{1,0:T(8,128)S(1)} %scatter_custom_fusion), channel_id=2, replica_groups=mesh['box'=8,'rep'=4] {'box'}, use_global_device_ids=true, to_apply=%region_4.5.clone | all-reduce | flops 10240 | bytes 81920
  53.1 30.7 %all-gather = bf16[8,20,64]{2,1,0:T(8,128)(2,1)S(1)} all-gather(bf16[1,20,64]{2,1,0:T(8,128)(2,1)S(1)} %get-tuple-element.23), channel_id=1, replica_groups=mesh['box'=8,'rep'=4] {'box'}, dimensions={0}, use_global_device_ids=true | all-gather | bytes 23040 | tf_op jit(solution)/shard_map/all_gather | solution.py:77
  83.8 0.1 copy.34
  83.9 0.1 reshape.72
  84.0 0.7 gather_fusion.1
  84.7 0.1 select_bitcast_fusion.1
  84.8 0.4 fusion.2
  85.3 0.1 reshape.64
  85.4 0.6 dynamic-slice
  86.7 0.6 gather_fusion
  87.4 0.1 fusion.12
  87.5 3.4 %fusion.10 = f32[16,1,256,1]{2,1,3,0:T(1,128)S(1)} fusion(bf16[16,2,256,256]{3,2,1,0:T(8,128)(2,1)} %param.11, bf16[16,2,256,1]{2,1,0,3:T(2,128)(2,1)S(1)} %fusion.12), kind=kOutput, calls=%fused_computation.22 | convolution fusion | flops 4194304 | bytes 4227072 | tf_op jit(solution)/shard_map/bsij,bsj->bi/dot_general | solution.py:58
  90.9 10.3 %all-reduce.4 = (f32[20,64]{1,0:T(8,128)S(1)}, f32[16,256]{1,0:T(8,128)S(1)}) all-reduce(f32[20,64]{1,0:T(8,128)S(1)} %dynamic-slice_add_fusion.1, f32[16,256]{1,0:T(8,128)S(1)} %fusion.15), channel_id=1, replica_groups=mesh['box'=8,'rep'=4] {'rep'}, use_global_device_ids=true, to_apply=%region_5.6 | all-reduce | flops 5376 | bytes 43008 | tf_op jit(solution)/shard_map/psum | solution.py:92
  101.2 0.6 gather_fusion.2
  101.7 0.2 fusion.43
  102.0 0.2 fusion.41
  102.2 0.6 multiply_reduce_fusion.2
  102.8 17.8 %all-reduce.2 = (f32[]{:T(128)}, f32[]{:T(128)}) all-reduce(f32[]{:T(128)} %get-tuple-element.3, f32[]{:T(128)} %get-tuple-element.2), channel_id=1, replica_groups=mesh['box'=8,'rep'=4] {'box'}, use_global_device_ids=true, to_apply=%region_1.2 | all-reduce | flops 2 | bytes 16 | tf_op jit(solution)/shard_map/psum | solution.py:47
  121.9 0.6 multiply_reduce_fusion.1
  122.5 19.7 %psum.60 = f32[]{:T(128)} all-reduce(f32[]{:T(128)} %get-tuple-element.10), channel_id=1, replica_groups=mesh['box'=8,'rep'=4] {'box'}, use_global_device_ids=true, to_apply=%region_9.10 | all-reduce | flops 1 | bytes 8 | tf_op jit(solution)/shard_map/psum | solution.py:47
  143.6 0.2 fusion.16
  143.9 1.3 collective-permute-start.2
  145.2 0.2 fusion.39
  145.3 0.1 convolution_convert_fusion
  145.5 0.3 fusion.29
  145.8 0.1 broadcast_multiply_fusion
  145.9 0.9 scatter_custom_fusion.1
  146.7 36.4 %all-reduce.1 = f32[160,64]{1,0:T(8,128)S(1)} all-reduce(f32[160,64]{1,0:T(8,128)S(1)} %scatter_custom_fusion.1), channel_id=3, replica_groups=mesh['box'=8,'rep'=4] {'box'}, use_global_device_ids=true, to_apply=%region_12.13.clone | all-reduce | flops 10240 | bytes 81920
  183.2 30.7 %all-gather.1 = bf16[8,20,64]{2,1,0:T(8,128)(2,1)S(1)} all-gather(bf16[1,20,64]{2,1,0:T(8,128)(2,1)S(1)} %get-tuple-element.21), channel_id=1, replica_groups=mesh['box'=8,'rep'=4] {'box'}, dimensions={0}, use_global_device_ids=true | all-gather | bytes 23040 | tf_op jit(solution)/shard_map/all_gather | solution.py:77
  213.9 0.7 gather_fusion.4
  214.5 0.1 select_bitcast_fusion
  214.6 0.4 fusion
  215.0 2.9 %fusion.18 = f32[16,1,2,256]{3,1,2,0:T(1,128)S(1)} fusion(bf16[16,2,256,256]{3,2,1,0:T(8,128)(2,1)} %param.11, bf16[16,256,1,1]{1,0,2,3:T(8,128)(2,1)S(1)} %bitcast.105), kind=kOutput, calls=%fused_computation.42 | convolution fusion | flops 4194304 | bytes 4235264 | tf_op jit(solution)/shard_map/bsij,bi->bsj/dot_general | solution.py:61
  218.0 0.1 fusion.25
  218.1 1.3 collective-permute-start.3
  219.5 0.6 gather_fusion.3
  220.1 0.1 fusion.13
  220.2 3.4 %fusion.8 = f32[16,1,256,1]{2,1,3,0:T(1,128)S(1)} fusion(bf16[16,2,256,256]{3,2,1,0:T(8,128)(2,1)} %param.11, bf16[16,2,256,1]{2,1,0,3:T(2,128)(2,1)S(1)} %fusion.13), kind=kOutput, calls=%fused_computation.19 | convolution fusion | flops 4194304 | bytes 4227072 | tf_op jit(solution)/shard_map/bsij,bsj->bi/dot_general | solution.py:58
  223.6 10.3 %all-reduce.3 = (f32[20,64]{1,0:T(8,128)S(1)}, f32[16,256]{1,0:T(8,128)S(1)}) all-reduce(f32[20,64]{1,0:T(8,128)S(1)} %dynamic-slice_add_fusion, f32[16,256]{1,0:T(8,128)S(1)} %fusion.14), channel_id=1, replica_groups=mesh['box'=8,'rep'=4] {'rep'}, use_global_device_ids=true, to_apply=%region_13.14 | all-reduce | flops 5376 | bytes 43008 | tf_op jit(solution)/shard_map/psum | solution.py:92
  233.9 0.6 gather_fusion.5
  234.5 0.2 fusion.37
  234.7 0.2 fusion.35
  234.9 0.6 multiply_reduce_fusion
  235.5 18.6 %psum.63 = f32[]{:T(128)} all-reduce(f32[]{:T(128)} %multiply_reduce_fusion), channel_id=1, replica_groups=mesh['box'=8,'rep'=4] {'box'}, use_global_device_ids=true, to_apply=%region_15.16 | all-reduce | flops 1 | bytes 8 | tf_op jit(solution)/shard_map/psum | solution.py:102
  255.5 0.6 multiply_subtract_fusion
  (61 shorter events, 0.5 us)
Async XLA Ops:
  0.6 11.7 %copy-start = (bf16[20,4,64,64]{3,2,1,0:T(8,128)(2,1)S(1)}, bf16[20,4,64,64]{3,2,1,0:T(8,128)(2,1)}, u32[]{:S(2)}) copy-start(bf16[20,4,64,64]{3,2,1,0:T(8,128)(2,1)} %param.16) | copy-start | bytes 1966084
  0.6 9.3 %copy-start.2 = (f32[16,256]{1,0:T(8,128)S(1)}, f32[16,256]{1,0:T(8,128)}, u32[]{:S(2)}) copy-start(f32[16,256]{1,0:T(8,128)} %param.9) | copy-start | bytes 49156
  0.7 3.8 %copy-start.5 = (s32[16,2]{0,1:T(2,128)S(1)}, s32[16,2]{0,1:T(2,128)}, u32[]{:S(2)}) copy-start(s32[16,2]{0,1:T(2,128)} %param.12) | copy-start | bytes 388
  0.7 10.6 %copy-start.1 = (bf16[16,64,256]{2,1,0:T(8,128)(2,1)S(1)}, bf16[16,64,256]{2,1,0:T(8,128)(2,1)}, u32[]{:S(2)}) copy-start(bf16[16,64,256]{2,1,0:T(8,128)(2,1)} %param.13) | copy-start | bytes 1572868
  0.7 10.9 %copy-start.4 = (s32[20,4]{0,1:T(4,128)S(1)}, s32[20,4]{0,1:T(4,128)}, u32[]{:S(2)}) copy-start(s32[20,4]{0,1:T(4,128)} %param.17) | copy-start | bytes 964
  0.7 11.3 %copy-start.7 = (bf16[16,64,64]{2,1,0:T(8,128)(2,1)S(1)}, bf16[16,64,64]{2,1,0:T(8,128)(2,1)}, u32[]{:S(2)}) copy-start(bf16[16,64,64]{2,1,0:T(8,128)(2,1)} %param.14) | copy-start | bytes 393220
  0.7 11.5 %copy-start.6 = (s32[16]{0:T(128)S(1)}, s32[16]{0:T(128)}, u32[]{:S(2)}) copy-start(s32[16]{0:T(128)} %param.15) | copy-start | bytes 196
  1.6 83.9 %copy-start.8 = (u32[32]{0:T(128)S(1)}, u32[32]{0:T(128)}, u32[]{:S(2)}) copy-start(u32[32]{0:T(128)} %constant.33) | copy-start | bytes 388
  5.1 85.8 %collective-permute-start.1 = (f32[16,256]{1,0:T(8,128)S(1)}, f32[16,256]{1,0:T(8,128)S(1)}, u32[]{:S(2)}, u32[]{:S(2)}) collective-permute-start(f32[16,256]{1,0:T(8,128)S(1)} %slice.47), channel_id=1, source_target_pairs={{0,4},{4,8},{8,12},{12,16},{16,20},{20,24},{24,28},{1,5},{5,9},{9,... | collective-permute-start | bytes 49160 | tf_op jit(solution)/shard_map/ppermute | solution.py:12
  10.0 76.8 %collective-permute-start = (bf16[16,256]{1,0:T(8,128)(2,1)S(1)}, bf16[16,256]{1,0:T(8,128)(2,1)S(1)}, u32[]{:S(2)}, u32[]{:S(2)}) collective-permute-start(bf16[16,256]{1,0:T(8,128)(2,1)S(1)} %convert_element_type.33), channel_id=1, source_target_pairs={{4,0},{8,4},{12,8},{16,12},{20,16},{24,20},{28,24},{5,1},{9,5},{13... | collective-permute-start | bytes 24584 | tf_op jit(solution)/shard_map/ppermute | solution.py:12
  12.6 89.6 %copy-start.3 = (f32[16,256]{1,0:T(8,128)S(1)}, f32[16,256]{1,0:T(8,128)}, u32[]{:S(2)}) copy-start(f32[16,256]{1,0:T(8,128)} %param.10) | copy-start | bytes 49156
  143.9 75.6 %collective-permute-start.2 = (bf16[16,256]{1,0:T(8,128)(2,1)S(1)}, bf16[16,256]{1,0:T(8,128)(2,1)S(1)}, u32[]{:S(2)}, u32[]{:S(2)}) collective-permute-start(bf16[16,256]{1,0:T(8,128)(2,1)S(1)} %fusion.57), channel_id=1, source_target_pairs={{4,0},{8,4},{12,8},{16,12},{20,16},{24,20},{28,24},{5,1},{9,5},{13... | collective-permute-start | bytes 24584 | tf_op jit(solution)/shard_map/ppermute | solution.py:12
  218.1 5.5 %collective-permute-start.3 = (f32[16,256]{1,0:T(8,128)S(1)}, f32[16,256]{1,0:T(8,128)S(1)}, u32[]{:S(2)}, u32[]{:S(2)}) collective-permute-start(f32[16,256]{1,0:T(8,128)S(1)} %slice.51), channel_id=1, source_target_pairs={{0,4},{4,8},{8,12},{12,16},{16,20},{20,24},{24,28},{1,5},{5,9},{9,... | collective-permute-start | bytes 49160 | tf_op jit(solution)/shard_map/ppermute | solution.py:12
where the time goes:
time: 257 us; the launch traced here: 256 us
  blocking collectives  214 us (83%)
  matrix products  16.1 us (6%)
  starting transfers between devices  8.75 us (3%)
  between operations  5.83 us (2%)
  other arithmetic  5.8 us (2%)
  local copies, waits for them, and re-layouts  5.68 us (2%)
    unnamed x2, blocking collectives  76 us
    all_gather x2, blocking collectives, local(): every_coef = lax.all_gather(node_coef, 'box', axis=0, tiled=True)  61.3 us
    psum x2, blocking collectives, squares(): return lax.psum(jnp.sum(vector * vector), 'box')  37.5 us
    psum x2, blocking collectives, local(): lax.psum((near_part, node_sums + far_forward), 'rep')  20.6 us
    psum x1, blocking collectives, local(): step_size = norm_now / lax.psum(jnp.sum(direction * image_vec), 'box')  18.6 us
    ppermute x4, starting transfers between devices, shifted(): return lax.ppermute(shard, axis, pairs)  8.75 us
    dot_general x2, matrix products, local(): jnp.einsum('bsij,bsj->bi', near_tiles, near_in, preferred_element_type=jn...  6.73 us
    dot_general x2, matrix products, local(): jnp.einsum('bsij,bi->bsj', near_tiles, rounded, preferred_element_type=jn...  5.7 us
  transfers between devices with their start and end apart: 4, of which 0 were waited for; matrix products, arithmetic and copies ran while one was open for 7% of the time, Pallas kernels for 0%

commit v1 on v0

--- a/solution.py
+++ b/solution.py
@@ -74,7 +74,15 @@
             jnp.bfloat16
         )
         node_coef = jnp.concatenate([leaf_coef, group_coef], axis=0)
-        every_coef = lax.all_gather(node_coef, "box", axis=0, tiled=True)
+        ways, here, step = (lax.axis_size("box"), lax.axis_index("box"), node_coef.shape[0])
+        line, have = (node_coef, 1)
+        while have < ways:
+            line = jnp.concatenate(
+                [line, lax.ppermute(line, "box", [(d, (d - have) % ways) for d in range(ways)])],
+                axis=0,
+            )
+            have = 2 * have
+        every_coef = jnp.roll(line, here * step, axis=0)
         partner_coef = jnp.where(far_valid[:, :, None], every_coef[far_index], bf_zero)
         far_forward = jnp.einsum(
             "nsab,nsb->na", coupling, partner_coef, preferred_element_type=jnp.float32

time: 257 us -> 210 us (0.82)
  blocking collectives: 214 us -> 147 us
  starting transfers between devices: 8.75 us -> 19.4 us
  waiting for transfers between devices: 0.01 us -> 4.28 us
  other arithmetic: 5.8 us -> 8.88 us
    all_gather x2 -> x0, blocking collectives: 61.3 us -> none  [local(): every_coef = lax.all_gather(node_coef, 'box', axis=0, tiled=True)]
    ppermute x0 -> x6, starting transfers between devices: none -> 11 us  [local(): lax.ppermute(line, 'box', [(d, (d - have) % ways) for d in range(ways)])]
    unnamed x2, blocking collectives: 76 us -> 70.8 us
    ppermute x0 -> x6, waiting for transfers between devices: none -> 4.27 us  [local(): lax.ppermute(line, 'box', [(d, (d - have) % ways) for d in range(ways)])]
  transfers between devices with their start and end apart: 4 -> 10, of which waited for: 0 -> 3; matrix products, arithmetic and copies ran while one was open for 7% -> 10% of each run, Pallas kernels for 0% -> 0%
where the time goes in v1:
time: 210 us; the launch traced here: 209 us
  blocking collectives  147 us (70%)
  starting transfers between devices  19.4 us (9%)
  matrix products  18 us (9%)
  other arithmetic  8.88 us (4%)
  local copies, waits for them, and re-layouts  5.94 us (3%)
  between operations  5.85 us (3%)
  waiting for transfers between devices  4.28 us (2%)
    unnamed x2, blocking collectives  70.8 us
    psum x2, blocking collectives, squares(): return lax.psum(jnp.sum(vector * vector), 'box')  37.5 us
    psum x2, blocking collectives, local(): lax.psum((near_part, node_sums + far_forward), 'rep')  20.6 us
    psum x1, blocking collectives, local(): step_size = norm_now / lax.psum(jnp.sum(direction * image_vec), 'box')  17.7 us
    ppermute x6, starting transfers between devices, local(): lax.ppermute(line, 'box', [(d, (d - have) % ways) for d in range(ways)])  11 us
    ppermute x4, starting transfers between devices, shifted(): return lax.ppermute(shard, axis, pairs)  8.42 us
    dot_general x2, matrix products, local(): jnp.einsum('bsij,bsj->bi', near_tiles, near_in, preferred_element_type=jn...  6.73 us
    dot_general x2, matrix products, local(): jnp.einsum('bsij,bi->bsj', near_tiles, rounded, preferred_element_type=jn...  5.68 us
  transfers between devices with their start and end apart: 10, of which 3 were waited for; matrix products, arithmetic and copies ran while one was open for 10% of the time, Pallas kernels for 0%

profile of v1, /device:TPU:0, one launch (start us, length us, event | category | flops | bytes accessed | tf_op | source)
XLA Modules:
  0.0 209.0 jit_solution(8238365426744272782)
XLA Ops:
  0.7 0.8 convert_bitcast_fusion.3
  1.5 1.3 fusion.22
  2.8 0.7 compare_select_fusion.2
  3.5 1.1 fusion.47
  4.6 0.1 convolution_convert_fusion.1
  4.7 6.1 %collective-permute-start.2 = (bf16[20,64]{1,0:T(8,128)(2,1)S(1)}, bf16[20,64]{1,0:T(8,128)(2,1)S(1)}, u32[]{:S(2)}, u32[]{:S(2)}) collective-permute-start(bf16[20,64]{1,0:T(8,128)(2,1)S(1)} %get-tuple-element.24), channel_id=1, source_target_pairs={{0,28},{4,0},{8,4},{12,8},{16,12},{20,16},{24,20},{28,24},{1,29},{... | collective-permute-start | bytes 7688 | tf_op jit(solution)/shard_map/ppermute | solution.py:81
  10.8 0.7 convert_bitcast_fusion.1
  11.5 0.7 broadcast_compare_fusion.1
  12.2 0.7 compare_select_fusion.1
  13.1 0.1 copy.27
  13.2 0.1 and.15
  13.3 2.8 %fusion.24 = f32[16,1,2,256]{3,1,2,0:T(1,128)S(1)} fusion(bf16[16,2,256,256]{3,2,1,0:T(8,128)(2,1)} %param.13, bf16[16,256,1,1]{1,0,2,3:T(8,128)(2,1)S(1)} %convert_bitcast_fusion.1), kind=kOutput, calls=%fused_computation.54 | convolution fusion | flops 4194304 | bytes 4235264 | tf_op jit(solution)/shard_map/bsij,bi->bsj/dot_general | solution.py:61
  16.2 0.1 fusion.29
  16.3 1.3 collective-permute-start.1
  17.6 1.3 collective-permute-start
  19.0 0.1 copy.34
  19.2 0.1 copy.32
  19.3 0.1 copy.31
  19.7 0.3 fusion.33
  20.1 0.9 scatter_custom_fusion
  21.0 4.7 %collective-permute-start.3 = (bf16[40,64]{1,0:T(8,128)(2,1)S(1)}, bf16[40,64]{1,0:T(8,128)(2,1)S(1)}, u32[]{:S(2)}, u32[]{:S(2)}) collective-permute-start(bf16[40,64]{1,0:T(8,128)(2,1)S(1)} %pad_maximum_fusion.4), channel_id=1, source_target_pairs={{0,24},{4,28},{8,0},{12,4},{16,8},{20,12},{24,16},{28,20},{1,25},{... | collective-permute-start | bytes 15368 | tf_op jit(solution)/shard_map/ppermute | solution.py:81
  25.7 33.9 %all-reduce = f32[160,64]{1,0:T(8,128)S(1)} all-reduce(f32[160,64]{1,0:T(8,128)S(1)} %scatter_custom_fusion), channel_id=2, replica_groups=mesh['box'=8,'rep'=4] {'box'}, use_global_device_ids=true, to_apply=%region_4.5.clone | all-reduce | flops 10240 | bytes 81920
  59.6 0.1 copy.33
  59.7 0.6 dynamic-slice
  61.1 0.6 gather_fusion
  61.8 3.4 %fusion.12 = f32[16,1,256,1]{2,1,3,0:T(1,128)S(1)} fusion(bf16[16,2,256,256]{3,2,1,0:T(8,128)(2,1)} %param.13, bf16[16,2,256,1]{2,1,0,3:T(2,128)(2,1)S(1)} %fusion.14), kind=kOutput, calls=%fused_computation.28 | convolution fusion | flops 4194304 | bytes 4227072 | tf_op jit(solution)/shard_map/bsij,bsj->bi/dot_general | solution.py:58
  65.2 0.5 collective-permute-done.4
  65.7 0.2 concatenate.43
  65.9 0.2 fusion.1
  66.1 0.7 gather_fusion.1
  66.8 0.4 fusion.4
  67.3 10.3 %all-reduce.4 = (f32[20,64]{1,0:T(8,128)S(1)}, f32[16,256]{1,0:T(8,128)S(1)}) all-reduce(f32[20,64]{1,0:T(8,128)S(1)} %dynamic-slice_add_fusion.1, f32[16,256]{1,0:T(8,128)S(1)} %fusion.17), channel_id=1, replica_groups=mesh['box'=8,'rep'=4] {'rep'}, use_global_device_ids=true, to_apply=%region_5.7 | all-reduce | flops 5376 | bytes 43008 | tf_op jit(solution)/shard_map/psum | solution.py:100
  77.6 0.6 gather_fusion.2
  78.2 0.2 fusion.45
  78.4 0.2 fusion.43
  78.6 0.6 multiply_reduce_fusion.2
  79.2 19.8 %all-reduce.2 = (f32[]{:T(128)}, f32[]{:T(128)}) all-reduce(f32[]{:T(128)} %get-tuple-element.4, f32[]{:T(128)} %get-tuple-element.3), channel_id=1, replica_groups=mesh['box'=8,'rep'=4] {'box'}, use_global_device_ids=true, to_apply=%region_1.2 | all-reduce | flops 2 | bytes 16 | tf_op jit(solution)/shard_map/psum | solution.py:47
  100.3 0.6 multiply_reduce_fusion.1
  100.9 17.7 %psum.60 = f32[]{:T(128)} all-reduce(f32[]{:T(128)} %get-tuple-element.11), channel_id=1, replica_groups=mesh['box'=8,'rep'=4] {'box'}, use_global_device_ids=true, to_apply=%region_9.11 | all-reduce | flops 1 | bytes 8 | tf_op jit(solution)/shard_map/psum | solution.py:47
  120.0 1.3 collective-permute-start.5
  121.3 0.2 fusion.18
  121.6 2.9 %fusion.20 = f32[16,1,2,256]{3,1,2,0:T(1,128)S(1)} fusion(bf16[16,2,256,256]{3,2,1,0:T(8,128)(2,1)} %param.13, bf16[16,256,1,1]{1,0,2,3:T(8,128)(2,1)S(1)} %bitcast.101), kind=kOutput, calls=%fused_computation.50 | convolution fusion | flops 4194304 | bytes 4235264 | tf_op jit(solution)/shard_map/bsij,bi->bsj/dot_general | solution.py:61
  124.5 0.1 fusion.27
  124.6 4.5 %collective-permute-start.6 = (f32[16,256]{1,0:T(8,128)S(1)}, f32[16,256]{1,0:T(8,128)S(1)}, u32[]{:S(2)}, u32[]{:S(2)}) collective-permute-start(f32[16,256]{1,0:T(8,128)S(1)} %slice.51), channel_id=1, source_target_pairs={{0,4},{4,8},{8,12},{12,16},{16,20},{20,24},{24,28},{1,5},{5,9},{9,... | collective-permute-start | bytes 49160 | tf_op jit(solution)/shard_map/ppermute | solution.py:12
  129.2 0.2 fusion.41
  129.4 0.1 convolution_convert_fusion
  129.6 0.3 fusion.31
  130.0 0.9 scatter_custom_fusion.1
  130.8 3.3 %collective-permute-done.7 = bf16[20,64]{1,0:T(8,128)(2,1)S(1)} collective-permute-done((bf16[20,64]{1,0:T(8,128)(2,1)S(1)}, bf16[20,64]{1,0:T(8,128)(2,1)S(1)}, u32[]{:S(2)}, u32[]{:S(2)}) %collective-permute-start.7) | collective-permute-done | bytes 2592 | tf_op jit(solution)/shard_map/ppermute | solution.py:81
  134.2 36.9 %all-reduce.1 = f32[160,64]{1,0:T(8,128)S(1)} all-reduce(f32[160,64]{1,0:T(8,128)S(1)} %scatter_custom_fusion.1), channel_id=3, replica_groups=mesh['box'=8,'rep'=4] {'box'}, use_global_device_ids=true, to_apply=%region_12.14.clone | all-reduce | flops 10240 | bytes 81920
  171.2 0.6 gather_fusion.3
  171.9 3.4 %fusion.10 = f32[16,1,256,1]{2,1,3,0:T(1,128)S(1)} fusion(bf16[16,2,256,256]{3,2,1,0:T(8,128)(2,1)} %param.13, bf16[16,2,256,1]{2,1,0,3:T(2,128)(2,1)S(1)} %fusion.15), kind=kOutput, calls=%fused_computation.25 | convolution fusion | flops 4194304 | bytes 4227072 | tf_op jit(solution)/shard_map/bsij,bsj->bi/dot_general | solution.py:58
  175.3 0.5 collective-permute-done.9
  175.8 0.2 concatenate.48
  176.0 0.2 fusion
  176.2 0.7 gather_fusion.4
  176.9 0.4 fusion.2
  177.4 10.3 %all-reduce.3 = (f32[20,64]{1,0:T(8,128)S(1)}, f32[16,256]{1,0:T(8,128)S(1)}) all-reduce(f32[20,64]{1,0:T(8,128)S(1)} %dynamic-slice_add_fusion, f32[16,256]{1,0:T(8,128)S(1)} %fusion.16), channel_id=1, replica_groups=mesh['box'=8,'rep'=4] {'rep'}, use_global_device_ids=true, to_apply=%region_13.15 | all-reduce | flops 5376 | bytes 43008 | tf_op jit(solution)/shard_map/psum | solution.py:100
  187.7 0.6 gather_fusion.5
  188.3 0.2 fusion.39
  188.5 0.2 fusion.37
  188.7 0.6 multiply_reduce_fusion
  189.3 17.7 %psum.63 = f32[]{:T(128)} all-reduce(f32[]{:T(128)} %multiply_reduce_fusion), channel_id=1, replica_groups=mesh['box'=8,'rep'=4] {'box'}, use_global_device_ids=true, to_apply=%region_15.17 | all-reduce | flops 1 | bytes 8 | tf_op jit(solution)/shard_map/psum | solution.py:110
  208.4 0.6 multiply_subtract_fusion
  (73 shorter events, 1.8 us)
Async XLA Ops:
  0.6 19.0 %copy-start = (bf16[20,4,64,64]{3,2,1,0:T(8,128)(2,1)S(1)}, bf16[20,4,64,64]{3,2,1,0:T(8,128)(2,1)}, u32[]{:S(2)}) copy-start(bf16[20,4,64,64]{3,2,1,0:T(8,128)(2,1)} %param.18) | copy-start | bytes 1966084
  0.6 59.1 %copy-start.6 = (u32[32]{0:T(128)S(1)}, u32[32]{0:T(128)}, u32[]{:S(2)}) copy-start(u32[32]{0:T(128)} %constant.49) | copy-start | bytes 388
  0.7 17.0 %copy-start.2 = (f32[16,256]{1,0:T(8,128)S(1)}, f32[16,256]{1,0:T(8,128)}, u32[]{:S(2)}) copy-start(f32[16,256]{1,0:T(8,128)} %param.11) | copy-start | bytes 49156
  0.7 18.3 %copy-start.4 = (s32[20,4]{0,1:T(4,128)S(1)}, s32[20,4]{0,1:T(4,128)}, u32[]{:S(2)}) copy-start(s32[20,4]{0,1:T(4,128)} %param.19) | copy-start | bytes 964
  4.7 16.2 %collective-permute-start.2 = (bf16[20,64]{1,0:T(8,128)(2,1)S(1)}, bf16[20,64]{1,0:T(8,128)(2,1)S(1)}, u32[]{:S(2)}, u32[]{:S(2)}) collective-permute-start(bf16[20,64]{1,0:T(8,128)(2,1)S(1)} %get-tuple-element.24), channel_id=1, source_target_pairs={{0,28},{4,0},{8,4},{12,8},{16,12},{20,16},{24,20},{28,24},{1,29},{... | collective-permute-start | bytes 7688 | tf_op jit(solution)/shard_map/ppermute | solution.py:81
  16.3 48.9 %collective-permute-start.1 = (f32[16,256]{1,0:T(8,128)S(1)}, f32[16,256]{1,0:T(8,128)S(1)}, u32[]{:S(2)}, u32[]{:S(2)}) collective-permute-start(f32[16,256]{1,0:T(8,128)S(1)} %slice.47), channel_id=1, source_target_pairs={{0,4},{4,8},{8,12},{12,16},{16,20},{20,24},{24,28},{1,5},{5,9},{9,... | collective-permute-start | bytes 49160 | tf_op jit(solution)/shard_map/ppermute | solution.py:12
  17.6 43.4 %collective-permute-start = (bf16[16,256]{1,0:T(8,128)(2,1)S(1)}, bf16[16,256]{1,0:T(8,128)(2,1)S(1)}, u32[]{:S(2)}, u32[]{:S(2)}) collective-permute-start(bf16[16,256]{1,0:T(8,128)(2,1)S(1)} %convert_element_type.33), channel_id=1, source_target_pairs={{4,0},{8,4},{12,8},{16,12},{20,16},{24,20},{28,24},{5,1},{9,5},{13... | collective-permute-start | bytes 24584 | tf_op jit(solution)/shard_map/ppermute | solution.py:12
  19.1 59.0 %copy-start.5 = (bf16[16,64,64]{2,1,0:T(8,128)(2,1)S(1)}, bf16[16,64,64]{2,1,0:T(8,128)(2,1)}, u32[]{:S(2)}) copy-start(bf16[16,64,64]{2,1,0:T(8,128)(2,1)} %param.16) | copy-start | bytes 393220
  19.7 58.7 %copy-start.1 = (bf16[16,64,256]{2,1,0:T(8,128)(2,1)S(1)}, bf16[16,64,256]{2,1,0:T(8,128)(2,1)}, u32[]{:S(2)}) copy-start(bf16[16,64,256]{2,1,0:T(8,128)(2,1)} %param.15) | copy-start | bytes 1572868
  20.0 58.6 %copy-start.3 = (f32[16,256]{1,0:T(8,128)S(1)}, f32[16,256]{1,0:T(8,128)}, u32[]{:S(2)}) copy-start(f32[16,256]{1,0:T(8,128)} %param.12) | copy-start | bytes 49156
  21.0 40.0 %collective-permute-start.3 = (bf16[40,64]{1,0:T(8,128)(2,1)S(1)}, bf16[40,64]{1,0:T(8,128)(2,1)S(1)}, u32[]{:S(2)}, u32[]{:S(2)}) collective-permute-start(bf16[40,64]{1,0:T(8,128)(2,1)S(1)} %pad_maximum_fusion.4), channel_id=1, source_target_pairs={{0,24},{4,28},{8,0},{12,4},{16,8},{20,12},{24,16},{28,20},{1,25},{... | collective-permute-start | bytes 15368 | tf_op jit(solution)/shard_map/ppermute | solution.py:81
  61.0 4.7 %collective-permute-start.4 = (bf16[80,64]{1,0:T(8,128)(2,1)S(1)}, bf16[80,64]{1,0:T(8,128)(2,1)S(1)}, u32[]{:S(2)}, u32[]{:S(2)}) collective-permute-start(bf16[80,64]{1,0:T(8,128)(2,1)S(1)} %pad_maximum_fusion), channel_id=1, source_target_pairs={{0,16},{4,20},{8,24},{12,28},{16,0},{20,4},{24,8},{28,12},{1,17},{... | collective-permute-start | bytes 30728 | tf_op jit(solution)/shard_map/ppermute | solution.py:81
  120.0 51.1 %collective-permute-start.5 = (bf16[16,256]{1,0:T(8,128)(2,1)S(1)}, bf16[16,256]{1,0:T(8,128)(2,1)S(1)}, u32[]{:S(2)}, u32[]{:S(2)}) collective-permute-start(bf16[16,256]{1,0:T(8,128)(2,1)S(1)} %fusion.55), channel_id=1, source_target_pairs={{4,0},{8,4},{12,8},{16,12},{20,16},{24,20},{28,24},{5,1},{9,5},{13... | collective-permute-start | bytes 24584 | tf_op jit(solution)/shard_map/ppermute | solution.py:12
  124.6 50.7 %collective-permute-start.6 = (f32[16,256]{1,0:T(8,128)S(1)}, f32[16,256]{1,0:T(8,128)S(1)}, u32[]{:S(2)}, u32[]{:S(2)}) collective-permute-start(f32[16,256]{1,0:T(8,128)S(1)} %slice.51), channel_id=1, source_target_pairs={{0,4},{4,8},{8,12},{12,16},{16,20},{20,24},{24,28},{1,5},{5,9},{9,... | collective-permute-start | bytes 49160 | tf_op jit(solution)/shard_map/ppermute | solution.py:12
  129.5 4.6 %collective-permute-start.7 = (bf16[20,64]{1,0:T(8,128)(2,1)S(1)}, bf16[20,64]{1,0:T(8,128)(2,1)S(1)}, u32[]{:S(2)}, u32[]{:S(2)}) collective-permute-start(bf16[20,64]{1,0:T(8,128)(2,1)S(1)} %get-tuple-element.22), channel_id=1, source_target_pairs={{0,28},{4,0},{8,4},{12,8},{16,12},{20,16},{24,20},{28,24},{1,29},{... | collective-permute-start | bytes 7688 | tf_op jit(solution)/shard_map/ppermute | solution.py:81
  134.1 37.0 %collective-permute-start.8 = (bf16[40,64]{1,0:T(8,128)(2,1)S(1)}, bf16[40,64]{1,0:T(8,128)(2,1)S(1)}, u32[]{:S(2)}, u32[]{:S(2)}) collective-permute-start(bf16[40,64]{1,0:T(8,128)(2,1)S(1)} %pad_maximum_fusion.5), channel_id=1, source_target_pairs={{0,24},{4,28},{8,0},{12,4},{16,8},{20,12},{24,16},{28,20},{1,25},{... | collective-permute-start | bytes 15368 | tf_op jit(solution)/shard_map/ppermute | solution.py:81
  171.1 4.7 %collective-permute-start.9 = (bf16[80,64]{1,0:T(8,128)(2,1)S(1)}, bf16[80,64]{1,0:T(8,128)(2,1)S(1)}, u32[]{:S(2)}, u32[]{:S(2)}) collective-permute-start(bf16[80,64]{1,0:T(8,128)(2,1)S(1)} %pad_maximum_fusion.1), channel_id=1, source_target_pairs={{0,16},{4,20},{8,24},{12,28},{16,0},{20,4},{24,8},{28,12},{1,17},{... | collective-permute-start | bytes 30728 | tf_op jit(solution)/shard_map/ppermute | solution.py:81
